TPU v7x, 256 devices: a whole 4x4x8 slice. The times are simulated.
256 devices in a mesh: src: 8 (over z_hi, y), width: 32 (over z_lo, x, core).
Axes of the slice: x: 4, y: 4, z: 8 (z_hi: 2, z_lo: 4; z = z_hi * 4 + z_lo), core: 2. Of those that a mesh axis runs over, the one named last changes fastest.
Arguments:
- resid: bfloat16 [8, 512, 8192], P('src', None, 'width'), may hold values from -6 to 6
- enc_w: bfloat16 [8, 8192, 6144], P('src', 'width'), may hold values from -0.0625 to 0.0625
- enc_b: float32 [8, 6144], P('src'), may hold values from -3 to 3
- dec_w: bfloat16 [8, 6144, 8192], P('src', None, 'width'), may hold values from -0.078125 to 0.078125
- target: bfloat16 [512, 8192], P(None, 'width'), may hold values from -36 to 36
- norm_gain: float32 [8192], P('width'), may hold values from 0.5 to 1.5
- wq: bfloat16 [8192, 8192], P(None, 'width'), may hold values from -0.0625 to 0.0625
- wk: bfloat16 [8192, 1024], P('width'), may hold values from -0.0625 to 0.0625
- wv: bfloat16 [8192, 1024], P('width'), may hold values from -0.0625 to 0.0625
- prompt_ids: int32 [512], replicated, may hold values from 0 to 3, never falling along the last dimension, each value on 1 to 256 neighbouring positions
Outputs:
- mlp_out: bfloat16 [512, 8192], P('src', 'width')
- context: bfloat16 [512, 8192], P('src', 'width')
Inputs may be any that keep to these rules, and one draw needn't show every extreme that they name: `prompt_ids`: rows of one prompt are contiguous and numbered in increasing order; the longest prompt has 256 rows.
All inputs are finite; a program needn't handle non-finite values.
Results may differ from a plain program's by a relative error of at most 0.008.
Values may be sent and summed in bfloat16 or wider, within the bound.
No kernel may reach another device: no remote copies, remote signals or barrier semaphores. Data moves between devices by JAX's collectives and lax.ppermute only.
A program may use at most 128 MiB of HBM per device.

v0:
```python
import math
import jax
import jax.numpy as jnp
from jax import lax
from jax.sharding import Mesh
from jax.sharding import PartitionSpec as P

HD = 128
GROUP = 8
WIDTH = ("wc", "core")
SWAP = [(0, 1), (1, 0)]


def contract0(a, b):
    return lax.dot_general(a, b, (((0,), (0,)), ((), ())), preferred_element_type=jnp.float32)


def on_device(resid, enc_w, enc_b, dec_w, target, norm_gain, wq, wk, wv, prompt_ids):
    n_wc = lax.axis_size("wc")
    n_core = lax.axis_size("core")
    n_src = lax.axis_size("src")
    core = lax.axis_index("core")
    chip = lax.axis_index("wc")
    src = lax.axis_index("src")
    width_pos = chip * n_core + core
    rows_all = resid.shape[1]
    width_local = resid.shape[2]
    width_all = width_local * n_wc * n_core
    feats_all = enc_w.shape[2]
    half = feats_all // 2
    share = half // n_wc
    other = 1 - core
    x = resid[0]
    we = enc_w[0]
    we_mine = lax.dynamic_slice_in_dim(we, core * half, half, 1)
    we_give = lax.dynamic_slice_in_dim(we, other * half, half, 1)
    we_got = lax.ppermute(we_give, "core", SWAP)
    x_got = lax.ppermute(x, "core", SWAP)
    pre = lax.dot_general(we_mine, x, (((0,), (1,)), ((), ())), preferred_element_type=jnp.float32)
    pre = pre + lax.dot_general(
        we_got, x_got, (((0,), (1,)), ((), ())), preferred_element_type=jnp.float32
    )
    pre_share = lax.psum_scatter(pre, "wc", scatter_dimension=0, tiled=True)
    bias = lax.dynamic_slice_in_dim(enc_b[0], core * half + chip * share, share, 0)
    feats_t = jnp.maximum(pre_share + bias[:, None], 0.0).astype(jnp.bfloat16)
    feats_half = lax.all_gather(feats_t, "wc", axis=0, tiled=True)
    wd = dec_w[0]
    wd_mine = lax.dynamic_slice_in_dim(wd, core * half, half, 0)
    wd_give = lax.dynamic_slice_in_dim(wd, other * half, half, 0)
    wd_got = lax.ppermute(wd_give, "core", SWAP)
    part_mine = contract0(feats_half, wd_mine)
    part_other = contract0(feats_half, wd_got)
    mlp_layer = part_mine + lax.ppermute(part_other, "core", SWAP)
    query_rows = rows_all // n_src
    row_start = src * query_rows
    mlp = lax.psum_scatter(mlp_layer, "src", scatter_dimension=0, tiled=True)
    mlp_out = mlp.astype(jnp.bfloat16)
    tgt = lax.dynamic_slice_in_dim(target, row_start, query_rows, 0)
    stream = tgt.astype(jnp.float32) + mlp
    stream_full = lax.all_gather(stream, WIDTH, axis=1, tiled=True)
    gain_full = lax.all_gather(norm_gain, WIDTH, axis=0, tiled=True)
    power = jnp.sum(stream_full * stream_full, axis=1) / width_all
    scale = lax.rsqrt(power + 1e-05)[:, None]
    normed_full = (stream_full * scale * gain_full[None, :]).astype(jnp.bfloat16)
    normed_loc = (stream * scale * norm_gain[None, :]).astype(jnp.bfloat16)
    query = jnp.dot(normed_full, wq, preferred_element_type=jnp.float32).astype(jnp.bfloat16)
    key_part = jnp.dot(normed_loc, wk, preferred_element_type=jnp.float32)
    value_part = jnp.dot(normed_loc, wv, preferred_element_type=jnp.float32)
    key_total, value_total = lax.psum((key_part, value_part), WIDTH)
    heads_here = wq.shape[1] // HD
    kv_index = width_pos * heads_here // GROUP
    key_head = lax.dynamic_slice_in_dim(key_total, kv_index * HD, HD, 1).astype(jnp.bfloat16)
    value_head = lax.dynamic_slice_in_dim(value_total, kv_index * HD, HD, 1).astype(jnp.bfloat16)
    key_head = lax.all_gather(key_head, "src", axis=0, tiled=True)
    value_head = lax.all_gather(value_head, "src", axis=0, tiled=True)
    query3 = query.reshape(query_rows, heads_here, HD)
    scores = jnp.einsum(
        "qhd,sd->hqs", query3, key_head, preferred_element_type=jnp.float32
    ) / math.sqrt(HD)
    query_index = row_start + jnp.arange(query_rows, dtype=jnp.int32)
    key_index = jnp.arange(rows_all, dtype=jnp.int32)
    query_prompt = lax.dynamic_slice_in_dim(prompt_ids, row_start, query_rows, 0)
    allowed = (query_prompt[:, None] == prompt_ids[None, :]) & (
        key_index[None, :] <= query_index[:, None]
    )
    scores = jnp.where(allowed[None], scores, -1e30)
    peak = jnp.max(scores, axis=-1, keepdims=True)
    weights = jnp.exp(scores - peak)
    probs = (weights / jnp.sum(weights, axis=-1, keepdims=True)).astype(jnp.bfloat16)
    context = jnp.einsum("hqs,sd->qhd", probs, value_head, preferred_element_type=jnp.float32)
    return (mlp_out, context.reshape(query_rows, heads_here * HD).astype(jnp.bfloat16))


def solution(mesh):
    n_src = mesh.shape["src"]
    n_width = mesh.shape["width"]
    fine = Mesh(mesh.devices.reshape(n_src, n_width // 2, 2), ("src", "wc", "core"))
    in_specs = (
        P("src", None, WIDTH),
        P("src", WIDTH, None),
        P("src", None),
        P("src", None, WIDTH),
        P(None, WIDTH),
        P(WIDTH),
        P(None, WIDTH),
        P(WIDTH, None),
        P(WIDTH, None),
        P(),
    )
    out_specs = (P("src", WIDTH), P("src", WIDTH))
    return jax.shard_map(
        on_device, mesh=fine, in_specs=in_specs, out_specs=out_specs, check_vma=False
    )
```

profile of v0, /device:TPU:24, one launch (start us, length us, event | category | flops | bytes accessed | tf_op | source)
XLA Modules:
  0.0 602.3 jit_solution(9003281034998828032)
XLA Ops:
  7.2 1.8 copy-done
  9.1 1.3 dynamic-slice_bitcast_fusion.1
  10.4 0.5 collective-permute-start.1
  10.9 1.0 fusion.3
  11.9 2.6 collective-permute-done.1
  14.5 5.2 convolution_add_fusion
  19.8 0.8 constant_dynamic-slice_fusion
  20.5 102.9 %reduce-scatter.3.cloned.1.call-done = f32[192,512]{1,0:T(8,128)} async-done(((f32[3072,512]{1,0:T(8,128)}), f32[192,512]{1,0:T(8,128)}) %reduce-scatter.3.cloned.1.call-update) | async-done | bytes 393232 | tf_op jit(solution)/shard_map/reduce_scatter | solution.py:43
  123.4 1.8 maximum_convert_fusion
  125.3 1.5 dynamic-slice_bitcast_fusion
  126.9 3.5 collective-permute-done.2
  130.4 76.5 %all-gather.4.cloned.1.call-done = bf16[3072,512]{1,0:T(8,128)(2,1)} async-done(((bf16[192,512]{1,0:T(8,128)(2,1)}), bf16[3072,512]{1,0:T(8,128)(2,1)}) %all-gather.4.cloned.1.call-update) | async-done | bytes 3145744 | tf_op jit(solution)/shard_map/all_gather | solution.py:46
  207.0 3.5 fusion.41
  210.6 2.4 fusion.1
  213.1 0.9 add.81
  214.0 83.6 %reduce-scatter.5.cloned.1.call-done = f32[64,256]{1,0:T(8,128)} async-done(((f32[512,256]{1,0:T(8,128)}), f32[64,256]{1,0:T(8,128)}) %reduce-scatter.5.cloned.1.call-update) | async-done | bytes 65552 | tf_op jit(solution)/shard_map/reduce_scatter | solution.py:56
  297.6 1.6 convert_add_fusion
  299.3 40.4 %all-gather = f32[32,1,256]{2,1,0:T(1,128)S(1)} all-gather(f32[1,1,256]{2,1,0:T(1,128)S(1)} %bitcast.66), channel_id=1, replica_groups=mesh['src'=8,'wc'=16,'core'=2] {'wc','core'}, dimensions={0}, use_global_device_ids=true | all-gather | bytes 33792 | tf_op jit(solution)/shard_map/all_gather | solution.py:61
  339.7 0.1 fusion.17
  339.8 15.4 %all-gather.6.cloned.1.call-done = f32[64,8192]{1,0:T(8,128)} async-done(((f32[64,256]{1,0:T(8,128)}), f32[64,8192]{1,0:T(8,128)}) %all-gather.6.cloned.1.call-update) | async-done | bytes 2097168 | tf_op jit(solution)/shard_map/all_gather | solution.py:60
  355.2 1.9 multiply_reduce_fusion
  357.1 1.3 fusion.34
  358.5 1.0 fusion.35
  359.4 140.9 %all-reduce.2 = (bf16[64,1024]{1,0:T(8,128)(2,1)}, bf16[64,1024]{1,0:T(8,128)(2,1)}) all-reduce(f32[64,1024]{1,0:T(8,128)} %fusion.35, f32[64,1024]{1,0:T(8,128)S(1)} %fusion.34), channel_id=1, replica_groups=mesh['src'=8,'wc'=16,'core'=2] {'wc','core'}, use_global_device_ids=true, to_apply=%region_3.0 | all-reduce | flops 131072 | bytes 786432 | tf_op jit(solution)/shard_map/psum | solution.py:69
  500.3 0.7 dynamic-slice_convert_fusion
  501.0 43.8 %all_gather.18 = bf16[512,128]{1,0:T(8,128)(2,1)S(1)} all-gather(bf16[64,128]{1,0:T(8,128)(2,1)S(1)} %dynamic-slice_convert_fusion), channel_id=1, replica_groups=mesh['src'=8,'wc'=16,'core'=2] {'src'}, dimensions={0}, use_global_device_ids=true | all-gather | bytes 147456 | tf_op jit(solution)/shard_map/all_gather | solution.py:74
  544.8 0.7 dynamic-slice_convert_fusion.1
  545.5 43.8 %all_gather.17 = bf16[512,128]{1,0:T(8,128)(2,1)S(1)} all-gather(bf16[64,128]{1,0:T(8,128)(2,1)S(1)} %dynamic-slice_convert_fusion.1), channel_id=1, replica_groups=mesh['src'=8,'wc'=16,'core'=2] {'src'}, dimensions={0}, use_global_device_ids=true | all-gather | bytes 147456 | tf_op jit(solution)/shard_map/all_gather | solution.py:75
  589.3 3.7 fusion.11
  593.0 1.0 fusion.36
  594.0 1.2 fusion.12
  595.2 0.6 copy.30
  (29 shorter events, 0.5 us)
Async XLA Ops:
  7.2 1.9 copy-start
  7.2 3.2 copy-start.4
  7.2 116.2 %reduce-scatter.3.cloned.1.call-start = ((), (), s32[]{:S(2)}) async-start(), calls=%async_computation.2 | async-start | bytes 6684672 | tf_op jit(solution)/shard_map/reduce_scatter | solution.py:43
  10.3 4.1 collective-permute-start
  10.4 4.1 collective-permute-start.1
  19.7 187.3 %all-gather.4.cloned.1.call-start = ((), (), s32[]{:S(2)}) async-start(), calls=%async_computation.3 | async-start | bytes 3342336 | tf_op jit(solution)/shard_map/all_gather | solution.py:46
  125.2 172.4 %reduce-scatter.5.cloned.1.call-start = ((), (), s32[]{:S(2)}) async-start(), calls=%async_computation.4 | async-start | bytes 589824 | tf_op jit(solution)/shard_map/reduce_scatter | solution.py:56
  126.8 3.6 collective-permute-start.2
  207.0 3.7 copy-start.1
  210.5 88.7 %copy-start.6 = (s32[512]{0:T(512)S(1)}, s32[512]{0:T(512)}, u32[]{:S(2)}) copy-start(s32[512]{0:T(512)} %param.19) | copy-start | bytes 6148
  210.5 88.8 %copy-start.5 = (f32[256]{0:T(256)S(1)}, f32[256]{0:T(256)}, u32[]{:S(2)}) copy-start(f32[256]{0:T(256)} %param.15) | copy-start | bytes 3076
  210.5 2.5 collective-permute-start.3
  214.0 141.2 %all-gather.6.cloned.1.call-start = ((), (), s32[]{:S(2)}) async-start(), calls=%async_computation.5 | async-start | bytes 2162688 | tf_op jit(solution)/shard_map/all_gather | solution.py:60
  299.2 59.3 %copy-start.2 = (f32[64,256]{1,0:T(8,128)S(1)}, f32[64,256]{1,0:T(8,128)}, u32[]{:S(2)}) copy-start(f32[64,256]{1,0:T(8,128)} %get-tuple-element.4) | copy-start | bytes 196612
  355.2 3.3 copy-start.3
Sparse Core Ops, SparseCore 0:
  19.8 103.5 reduce-scatter.2
  125.4 81.5 all-gather.3
  214.1 83.4 reduce-scatter.4
  299.3 55.8 all-gather.5
where the time goes:
time: 603 us; the launch traced here: 602 us
  waiting for transfers between devices  285 us (47%)
  blocking collectives  269 us (45%)
  matrix products  20.3 us (3%)
  between operations  14 us (2%)
  local copies, waits for them, and re-layouts  7.55 us (1%)
  other arithmetic  6.22 us (1%)
    psum x1, blocking collectives, on_device(): key_total, value_total = lax.psum((key_part, value_part), WIDTH)  141 us
    reduce_scatter x1, waiting for transfers between devices, on_device(): pre_share = lax.psum_scatter(pre, 'wc', scatter_dimension=0, tiled=True)  103 us
    reduce_scatter x1, waiting for transfers between devices, on_device(): mlp = lax.psum_scatter(mlp_layer, 'src', scatter_dimension=0, tiled=True)  83.6 us
    all_gather x1, waiting for transfers between devices, on_device(): feats_half = lax.all_gather(feats_t, 'wc', axis=0, tiled=True)  76.5 us
    all_gather x1, blocking collectives, on_device(): key_head = lax.all_gather(key_head, 'src', axis=0, tiled=True)  43.8 us
    all_gather x1, blocking collectives, on_device(): value_head = lax.all_gather(value_head, 'src', axis=0, tiled=True)  43.8 us
    all_gather x1, blocking collectives, on_device(): gain_full = lax.all_gather(norm_gain, WIDTH, axis=0, tiled=True)  40.4 us
    all_gather x1, waiting for transfers between devices, on_device(): stream_full = lax.all_gather(stream, WIDTH, axis=1, tiled=True)  15.4 us
  transfers between devices with their start and end apart: 8, of which 6 were waited for; matrix products, arithmetic and copies ran while one was open for 1% of the time, Pallas kernels for 0%

commit v1 on v0

--- a/solution.py
+++ b/solution.py
@@ -1,3 +1,4 @@
+import functools
 import math
 import jax
 import jax.numpy as jnp
@@ -9,6 +10,16 @@
 GROUP = 8
 WIDTH = ("wc", "core")
 SWAP = [(0, 1), (1, 0)]
+
+
+def read_positions(z, dim_i):
+    return jnp.concatenate(
+        lax.all_to_all(jnp.stack([z for _ in range(lax.axis_size("src"))], axis=0), "src", 0, 0),
+        axis=dim_i,
+    )
+
+
+forms_recover = functools.partial(read_positions, dim_i=0)
 
 
 def contract0(a, b):
@@ -72,7 +83,7 @@
     key_head = lax.dynamic_slice_in_dim(key_total, kv_index * HD, HD, 1).astype(jnp.bfloat16)
     value_head = lax.dynamic_slice_in_dim(value_total, kv_index * HD, HD, 1).astype(jnp.bfloat16)
     key_head = lax.all_gather(key_head, "src", axis=0, tiled=True)
-    value_head = lax.all_gather(value_head, "src", axis=0, tiled=True)
+    value_head = forms_recover(value_head)
     query3 = query.reshape(query_rows, heads_here, HD)
     scores = jnp.einsum(
         "qhd,sd->hqs", query3, key_head, preferred_element_type=jnp.float32

time: 603 us -> 573 us (0.950)
  blocking collectives: 269 us -> 225 us
  starting transfers between devices: 0.86 us -> 9.19 us
    all_gather x1 -> x0, blocking collectives: 43.8 us -> none  [on_device(): value_head = lax.all_gather(value_head, 'src', axis=0, tiled=True)]
    all_to_all x0 -> x1, starting transfers between devices: none -> 8.34 us  [read_positions(): lax.all_to_all(jnp.stack([z for _ in range(lax.axis_size('src'))], axis=0...]
  transfers between devices with their start and end apart: 8 -> 9, of which waited for: 6 -> 7; matrix products, arithmetic and copies ran while one was open for 1% -> 2% of each run, Pallas kernels for 0% -> 0%
where the time goes in v1:
time: 573 us; the launch traced here: 571 us
  waiting for transfers between devices  288 us (50%)
  blocking collectives  225 us (39%)
  matrix products  20.3 us (4%)
  between operations  14 us (2%)
  starting transfers between devices  9.19 us (2%)
  local copies, waits for them, and re-layouts  8.22 us (1%)
  other arithmetic  6.21 us (1%)
    psum x1, blocking collectives, on_device(): key_total, value_total = lax.psum((key_part, value_part), WIDTH)  141 us
    reduce_scatter x1, waiting for transfers between devices, on_device(): pre_share = lax.psum_scatter(pre, 'wc', scatter_dimension=0, tiled=True)  103 us
    reduce_scatter x1, waiting for transfers between devices, on_device(): mlp = lax.psum_scatter(mlp_layer, 'src', scatter_dimension=0, tiled=True)  83.5 us
    all_gather x1, waiting for transfers between devices, on_device(): feats_half = lax.all_gather(feats_t, 'wc', axis=0, tiled=True)  76.5 us
    all_gather x1, blocking collectives, on_device(): key_head = lax.all_gather(key_head, 'src', axis=0, tiled=True)  43.8 us
    all_gather x1, blocking collectives, on_device(): gain_full = lax.all_gather(norm_gain, WIDTH, axis=0, tiled=True)  40.3 us
    all_gather x1, waiting for transfers between devices, on_device(): stream_full = lax.all_gather(stream, WIDTH, axis=1, tiled=True)  15.4 us
  transfers between devices with their start and end apart: 9, of which 7 were waited for; matrix products, arithmetic and copies ran while one was open for 2% of the time, Pallas kernels for 0%

profile of v1, /device:TPU:24, one launch (start us, length us, event | category | flops | bytes accessed | tf_op | source)
XLA Modules:
  0.0 571.2 jit_solution(13680922883425691608)
XLA Ops:
  7.2 1.8 copy-done
  9.1 1.3 dynamic-slice_bitcast_fusion.1
  10.9 1.0 fusion.3
  11.9 2.6 collective-permute-done.1
  14.5 5.2 convolution_add_fusion
  19.8 0.8 constant_dynamic-slice_fusion
  20.5 103.0 %reduce-scatter.3.cloned.1.call-done = f32[192,512]{1,0:T(8,128)} async-done(((f32[3072,512]{1,0:T(8,128)}), f32[192,512]{1,0:T(8,128)}) %reduce-scatter.3.cloned.1.call-update) | async-done | bytes 393232 | tf_op jit(solution)/shard_map/reduce_scatter | solution.py:54
  123.5 1.8 maximum_convert_fusion
  125.4 1.5 dynamic-slice_bitcast_fusion
  127.0 3.5 collective-permute-done.2
  130.5 76.5 %all-gather.4.cloned.1.call-done = bf16[3072,512]{1,0:T(8,128)(2,1)} async-done(((bf16[192,512]{1,0:T(8,128)(2,1)}), bf16[3072,512]{1,0:T(8,128)(2,1)}) %all-gather.4.cloned.1.call-update) | async-done | bytes 3145744 | tf_op jit(solution)/shard_map/all_gather | solution.py:57
  207.1 3.5 fusion.40
  210.7 2.4 fusion.1
  213.2 0.9 add.81
  214.1 83.5 %reduce-scatter.5.cloned.1.call-done = f32[64,256]{1,0:T(8,128)} async-done(((f32[512,256]{1,0:T(8,128)}), f32[64,256]{1,0:T(8,128)}) %reduce-scatter.5.cloned.1.call-update) | async-done | bytes 65552 | tf_op jit(solution)/shard_map/reduce_scatter | solution.py:67
  297.6 1.6 convert_add_fusion
  299.3 40.3 %all-gather = f32[32,1,256]{2,1,0:T(1,128)S(1)} all-gather(f32[1,1,256]{2,1,0:T(1,128)S(1)} %bitcast.68), channel_id=1, replica_groups=mesh['src'=8,'wc'=16,'core'=2] {'wc','core'}, dimensions={0}, use_global_device_ids=true | all-gather | bytes 33792 | tf_op jit(solution)/shard_map/all_gather | solution.py:72
  339.8 15.4 %all-gather.6.cloned.1.call-done = f32[64,8192]{1,0:T(8,128)} async-done(((f32[64,256]{1,0:T(8,128)}), f32[64,8192]{1,0:T(8,128)}) %all-gather.6.cloned.1.call-update) | async-done | bytes 2097168 | tf_op jit(solution)/shard_map/all_gather | solution.py:71
  355.1 1.9 multiply_reduce_fusion
  357.0 1.3 fusion.33
  358.4 0.9 fusion.34
  359.3 140.9 %all-reduce.2 = (bf16[64,1024]{1,0:T(8,128)(2,1)}, bf16[64,1024]{1,0:T(8,128)(2,1)}) all-reduce(f32[64,1024]{1,0:T(8,128)} %fusion.34, f32[64,1024]{1,0:T(8,128)S(1)} %fusion.33), channel_id=1, replica_groups=mesh['src'=8,'wc'=16,'core'=2] {'wc','core'}, use_global_device_ids=true, to_apply=%region_3.0 | all-reduce | flops 131072 | bytes 786432 | tf_op jit(solution)/shard_map/psum | solution.py:80
  500.2 0.7 dynamic-slice_convert_fusion
  501.0 43.8 %all_gather.14 = bf16[512,128]{1,0:T(8,128)(2,1)S(1)} all-gather(bf16[64,128]{1,0:T(8,128)(2,1)S(1)} %dynamic-slice_convert_fusion), channel_id=1, replica_groups=mesh['src'=8,'wc'=16,'core'=2] {'src'}, dimensions={0}, use_global_device_ids=true | all-gather | bytes 147456 | tf_op jit(solution)/shard_map/all_gather | solution.py:85
  544.7 0.7 dynamic-slice_convert_fusion.1
  545.5 0.7 stack.2
  546.1 8.3 %all-to-all-start = ((bf16[8,64,128]{2,1,0:T(8,128)(2,1)}), bf16[8,64,128]{2,1,0:T(8,128)(2,1)S(1)}, u32[]{:S(2)}, u32[]{:S(2)}) async-start(bf16[8,64,128]{2,1,0:T(8,128)(2,1)} %stack.2), calls=%async_computation.2 | async-start | bytes 262144 | tf_op jit(solution)/shard_map/all_to_all | solution.py:17
  554.5 3.7 fusion.11
  558.2 1.0 fusion.35
  559.2 3.7 all-to-all-done
  562.8 1.2 fusion.12
  564.0 0.6 copy.30
  (31 shorter events, 1.1 us)
Async XLA Ops:
  7.2 1.9 copy-start
  7.2 3.2 copy-start.4
  7.2 116.3 %reduce-scatter.3.cloned.1.call-start = ((), (), s32[]{:S(2)}) async-start(), calls=%async_computation.3 | async-start | bytes 6684672 | tf_op jit(solution)/shard_map/reduce_scatter | solution.py:54
  10.3 4.1 collective-permute-start
  10.4 4.1 collective-permute-start.1
  19.7 187.4 %all-gather.4.cloned.1.call-start = ((), (), s32[]{:S(2)}) async-start(), calls=%async_computation.4 | async-start | bytes 3342336 | tf_op jit(solution)/shard_map/all_gather | solution.py:57
  125.3 172.3 %reduce-scatter.5.cloned.1.call-start = ((), (), s32[]{:S(2)}) async-start(), calls=%async_computation.5 | async-start | bytes 589824 | tf_op jit(solution)/shard_map/reduce_scatter | solution.py:67
  126.9 3.6 collective-permute-start.2
  207.1 3.6 copy-start.1
  210.6 88.6 %copy-start.6 = (s32[512]{0:T(512)S(1)}, s32[512]{0:T(512)}, u32[]{:S(2)}) copy-start(s32[512]{0:T(512)} %param.19) | copy-start | bytes 6148
  210.6 88.7 %copy-start.5 = (f32[256]{0:T(256)S(1)}, f32[256]{0:T(256)}, u32[]{:S(2)}) copy-start(f32[256]{0:T(256)} %param.15) | copy-start | bytes 3076
  210.6 2.5 collective-permute-start.3
  214.1 141.1 %all-gather.6.cloned.1.call-start = ((), (), s32[]{:S(2)}) async-start(), calls=%async_computation.6 | async-start | bytes 2162688 | tf_op jit(solution)/shard_map/all_gather | solution.py:71
  299.2 59.2 %copy-start.2 = (f32[64,256]{1,0:T(8,128)S(1)}, f32[64,256]{1,0:T(8,128)}, u32[]{:S(2)}) copy-start(f32[64,256]{1,0:T(8,128)} %get-tuple-element.4) | copy-start | bytes 196612
  355.1 3.3 copy-start.3
  546.1 16.7 %all-to-all-start = ((bf16[8,64,128]{2,1,0:T(8,128)(2,1)}), bf16[8,64,128]{2,1,0:T(8,128)(2,1)S(1)}, u32[]{:S(2)}, u32[]{:S(2)}) async-start(bf16[8,64,128]{2,1,0:T(8,128)(2,1)} %stack.2), calls=%async_computation.2 | async-start | bytes 262144 | tf_op jit(solution)/shard_map/all_to_all | solution.py:17
Sparse Core Ops, SparseCore 0:
  19.8 103.6 reduce-scatter.2
  125.5 81.5 all-gather.3
  214.2 83.3 reduce-scatter.4
  299.3 55.7 all-gather.5
